TPU v7x, 512 devices: a whole 4x8x8 slice. The times are simulated.
512 devices in a mesh: req: 64 (over x, z, core), ch: 8 (over y).
Axes of the slice: x: 4, y: 8, z: 8, core: 2. Of those that a mesh axis runs over, the one named last changes fastest.
Arguments:
- tokens: bfloat16 [128, 4096], P('req', 'ch'), may hold values from -80 to 80
- attn_gain: float32 [4096], P('ch'), may hold values from 0.1 to 1.9
- w_query: bfloat16 [4096, 4096], P('ch', 'req'), may hold values from -0.09375 to 0.09375
- w_keyval: bfloat16 [4096, 512], P('ch', 'req'), may hold values from -0.09375 to 0.09375
- cache: bfloat16 [2, 128, 256, 2048], P(None, 'req', 'ch'), may hold values from -70 to 70
- lengths: int32 [128], P('req'), may hold values from 1 to 2047, as said below
- write_pos: int32 [128], P('req'), may hold values from 0 to 2047
- w_out: bfloat16 [4096, 4096], P('ch', 'req'), may hold values from -0.09375 to 0.09375
- mlp_gain: float32 [4096], P('ch'), may hold values from 0.1 to 1.9
- w_gate_up: bfloat16 [4096, 24576], P('ch', 'req'), may hold values from -0.09375 to 0.09375
- w_down: bfloat16 [12288, 4096], P('req', 'ch'), may hold values from -0.0546875 to 0.0546875
Outputs:
- layer_out: bfloat16 [128, 4096], P('req', 'ch')
- kv_new: bfloat16 [128, 512], P('req', 'ch')
Inputs may be any that keep to these rules, and one draw needn't show every extreme that they name: lengths[b] earlier tokens of request b are in the cache; the largest equals 2047 in every draw. The new token of request b goes to slot write_pos[b]; its earlier tokens fill the slots before it, going back cyclically.
All inputs are finite; a program needn't handle non-finite values.
Results may differ from a plain program's by a relative error of at most 0.0064.
Values may be sent and summed in bfloat16 or wider, within the bound.
No kernel may reach another device: no remote copies, remote signals or barrier semaphores. Data moves between devices by JAX's collectives and lax.ppermute only.
A program may use at most 64 MiB of HBM per device.

v0:
```python
import math
import jax
import jax.numpy as jnp
from jax import lax
from jax.sharding import PartitionSpec as P

D = 4096
H = 16
HD = 256
EPSILON = 1e-06


def rms_norm(values, gain):
    wide = values.astype(jnp.float32)
    squares = jnp.sum(wide * wide, axis=1)
    summed = lax.psum(squares, "ch")
    meansq = summed / D
    return (wide * lax.rsqrt(meansq + EPSILON)[:, None] * gain[None, :]).astype(jnp.bfloat16)


def body(
    tokens,
    attn_gain,
    w_query,
    w_keyval,
    cache,
    lengths,
    write_pos,
    w_out,
    mlp_gain,
    w_gate_up,
    w_down,
):
    rows = tokens.shape[0]
    chan = cache.shape[2]
    window = cache.shape[3]
    factor = 1.0 / math.sqrt(HD)
    normed = rms_norm(tokens, attn_gain)
    joined = jnp.concatenate([w_query, w_keyval], axis=1)
    head_parts = jnp.dot(
        lax.all_gather(normed, "req", axis=0, tiled=True),
        joined,
        preferred_element_type=jnp.float32,
    )
    query_cols = w_query.shape[1]
    query_part, keyval_part = (
        lax.all_to_all(head_parts[:, :query_cols], "req", split_axis=0, concat_axis=1, tiled=True),
        lax.all_to_all(head_parts[:, query_cols:], "req", split_axis=0, concat_axis=1, tiled=True),
    )
    query_sum, keyval_sum = (
        lax.psum_scatter(query_part, "ch", scatter_dimension=1, tiled=True),
        lax.psum_scatter(keyval_part, "ch", scatter_dimension=1, tiled=True),
    )
    queries = query_sum.astype(jnp.bfloat16).reshape(rows, H, chan)
    keyval_new = keyval_sum.astype(jnp.bfloat16)
    key_new = keyval_new[:, :chan]
    value_new = keyval_new[:, chan:]
    keys = cache[0]
    values_cache = cache[1]
    own_part = jnp.sum(
        queries.astype(jnp.float32) * key_new.astype(jnp.float32)[:, None, :], axis=-1
    )
    score_part = jnp.einsum("bhe,bew->bhw", queries, keys, preferred_element_type=jnp.float32)
    summed, own_sum = lax.psum((score_part, own_part), "ch")
    slot_index = jnp.arange(window, dtype=jnp.int32)
    offset = (write_pos[:, None] - 1 - slot_index[None, :]) % window
    usable = offset < lengths[:, None]
    scores = jnp.where(usable[:, None, :], summed * factor, -jnp.inf)
    own_score = own_sum * factor
    top = jnp.maximum(jnp.max(scores, axis=-1), own_score)
    weights = jnp.exp(scores - top[..., None])
    own_weight = jnp.exp(own_score - top)
    total = jnp.sum(weights, axis=-1) + own_weight
    weights_low = weights.astype(jnp.bfloat16)
    numer = jnp.einsum(
        "bhw,bew->bhe", weights_low, values_cache, preferred_element_type=jnp.float32
    )
    numer = (
        numer
        + own_weight.astype(jnp.bfloat16).astype(jnp.float32)[..., None]
        * value_new.astype(jnp.float32)[:, None, :]
    )
    attn_local = (numer / total[..., None]).astype(jnp.bfloat16).reshape(rows, H * chan)
    out_parts = jnp.dot(
        lax.all_gather(attn_local, "req", axis=0, tiled=True),
        w_out,
        preferred_element_type=jnp.float32,
    )
    out_part = lax.all_to_all(out_parts, "req", split_axis=0, concat_axis=1, tiled=True)
    out_sum = lax.psum_scatter(out_part, "ch", scatter_dimension=1, tiled=True)
    first = (tokens.astype(jnp.float32) + out_sum).astype(jnp.bfloat16)
    normed_two = rms_norm(first, mlp_gain)
    hidden_cols = w_gate_up.shape[1] // 2
    ffn_parts = jnp.dot(
        lax.all_gather(normed_two, "req", axis=0, tiled=True),
        w_gate_up,
        preferred_element_type=jnp.float32,
    )
    ffn_total = lax.psum(ffn_parts, "ch")
    hidden = (
        jax.nn.gelu(ffn_total[:, :hidden_cols], approximate=True) * ffn_total[:, hidden_cols:]
    ).astype(jnp.bfloat16)
    down_sum = lax.psum_scatter(
        jnp.dot(hidden, w_down, preferred_element_type=jnp.float32),
        "req",
        scatter_dimension=0,
        tiled=True,
    )
    layer_out = (first.astype(jnp.float32) + down_sum).astype(jnp.bfloat16)
    return (layer_out, keyval_new)


def solution(mesh):
    placed = (
        P("req", "ch"),
        P("ch"),
        P("ch", "req"),
        P("ch", "req"),
        P(None, "req", "ch", None),
        P("req"),
        P("req"),
        P("ch", "req"),
        P("ch"),
        P("ch", "req"),
        P("req", "ch"),
    )
    return jax.shard_map(
        body,
        mesh=mesh,
        in_specs=placed,
        out_specs=(P("req", "ch"), P("req", "ch")),
        check_vma=False,
    )
```

profile of v0, /device:TPU:1, one launch (start us, length us, event | category | flops | bytes accessed | tf_op | source)
XLA Modules:
  0.0 728.1 jit_solution(11447148937282177522)
XLA Ops:
  7.2 0.8 fusion.36
  8.0 14.7 %psum.35 = f32[2]{0:T(128)S(1)} all-reduce(f32[2]{0:T(128)S(1)} %fusion.36), channel_id=1, replica_groups=mesh['req'=64,'ch'=8] {'ch'}, use_global_device_ids=true, to_apply=%region_1.0 | all-reduce | flops 2 | bytes 16 | tf_op jit(solution)/shard_map/psum | solution.py:16
  23.5 60.2 %all-gather = bf16[64,2,512]{2,1,0:T(2,128)(2,1)S(1)} all-gather(bf16[1,2,512]{2,1,0:T(2,128)(2,1)S(1)} %fusion.45), channel_id=1, replica_groups=mesh['req'=64,'ch'=8] {'req'}, dimensions={0}, use_global_device_ids=true | all-gather | bytes 133120 | tf_op jit(solution)/shard_map/all_gather | solution.py:41
  83.7 1.0 fusion.24
  85.5 5.6 all-to-all-start.1
  91.9 8.9 %all-to-all-done.1 = f32[64,2,8]{2,1,0:T(2,128)S(1)} async-done(((f32[64,2,8]{2,1,0:T(2,128)}), f32[64,2,8]{2,1,0:T(2,128)S(1)}, u32[]{:S(2)}, u32[]{:S(2)}) %all-to-all-start.1) | async-done | bytes 4128 | tf_op jit(solution)/shard_map/all_to_all | solution.py:48
  100.8 4.4 all-to-all-start
  105.2 1.2 copy.40
  107.2 7.5 %all-to-all-done = f32[64,1,128]{2,1,0:T(1,128)S(1)} async-done(((f32[64,1,128]{2,1,0:T(1,128)}), f32[64,1,128]{2,1,0:T(1,128)S(1)}, u32[]{:S(2)}, u32[]{:S(2)}) %all-to-all-start) | async-done | bytes 32800 | tf_op jit(solution)/shard_map/all_to_all | solution.py:47
  116.0 2.0 copy.39
  118.2 23.1 %reduce-scatter.12.cloned.1.call-done = f32[64,2]{1,0:T(8,128)} async-done(((f32[512,2]{1,0:T(8,128)}), f32[64,2]{1,0:T(8,128)}) %reduce-scatter.12.cloned.1.call-update) | async-done | bytes 528
  142.2 47.1 %reduce-scatter.10.cloned.1.call-done = f32[512,2]{1,0:T(8,128)} async-done(((f32[4096,2]{1,0:T(8,128)}), f32[512,2]{1,0:T(8,128)}) %reduce-scatter.10.cloned.1.call-update) | async-done | bytes 4112
  189.3 1.1 copy.34
  190.5 0.9 fusion.3
  191.6 11.9 %psum.37 = f32[2,16]{1,0:T(2,128)S(1)} all-reduce(f32[2,16]{1,0:T(2,128)S(1)} %multiply_reduce_fusion), channel_id=1, replica_groups=mesh['req'=64,'ch'=8] {'ch'}, use_global_device_ids=true, to_apply=%region_7.8 | all-reduce | flops 32 | bytes 256 | tf_op jit(solution)/shard_map/psum | solution.py:64
  203.5 64.4 %all-reduce.5.cloned.1.call-done = f32[2,16,2048]{2,1,0:T(8,128)} async-done(((f32[2,16,2048]{2,1,0:T(8,128)}), f32[2,16,2048]{2,1,0:T(8,128)}) %all-reduce.5.cloned.1.call-update) | async-done | bytes 262160 | tf_op jit(solution)/shard_map/psum | solution.py:64
  267.9 1.1 fusion.7
  269.0 1.2 fusion.8
  270.1 1.2 fusion.1
  271.4 57.0 %all-gather.1 = bf16[64,2,512]{2,1,0:T(2,128)(2,1)S(1)} all-gather(bf16[1,2,512]{2,1,0:T(2,128)(2,1)S(1)} %reshape.73), channel_id=1, replica_groups=mesh['req'=64,'ch'=8] {'req'}, dimensions={0}, use_global_device_ids=true | all-gather | bytes 133120 | tf_op jit(solution)/shard_map/all_gather | solution.py:85
  328.8 16.1 %all_to_all.57 = f32[64,1,128]{2,1,0:T(1,128)S(1)} all-to-all(f32[64,1,128]{2,1,0:T(1,128)S(1)} %reshape.87), channel_id=1, replica_groups=mesh['req'=64,'ch'=8] {'req'}, dimensions={0} | all-to-all | bytes 65536 | tf_op jit(solution)/shard_map/all_to_all | solution.py:89
  345.8 2.0 copy.41
  347.9 32.4 %reduce-scatter.14.cloned.1.call-done = f32[512,2]{1,0:T(8,128)} async-done(((f32[4096,2]{1,0:T(8,128)}), f32[512,2]{1,0:T(8,128)}) %reduce-scatter.14.cloned.1.call-update) | async-done | bytes 4112
  380.3 1.1 copy.38
  381.5 12.0 %psum.38 = f32[2]{0:T(128)S(1)} all-reduce(f32[2]{0:T(128)S(1)} %get-tuple-element.2), channel_id=1, replica_groups=mesh['req'=64,'ch'=8] {'ch'}, use_global_device_ids=true, to_apply=%region_11.12 | all-reduce | flops 2 | bytes 16 | tf_op jit(solution)/shard_map/psum | solution.py:16
  393.6 59.6 %all-gather.2 = bf16[64,2,512]{2,1,0:T(2,128)(2,1)S(1)} all-gather(bf16[1,2,512]{2,1,0:T(2,128)(2,1)S(1)} %fusion.44), channel_id=1, replica_groups=mesh['req'=64,'ch'=8] {'req'}, dimensions={0}, use_global_device_ids=true | all-gather | bytes 133120 | tf_op jit(solution)/shard_map/all_gather | solution.py:95
  453.2 0.9 fusion.56
  454.2 69.2 %all-reduce.7.cloned.1.call-done = f32[128,384]{1,0:T(8,128)} async-done(((f32[128,384]{1,0:T(8,128)}), f32[128,384]{1,0:T(8,128)}) %all-reduce.7.cloned.1.call-update) | async-done | bytes 196624 | tf_op jit(solution)/shard_map/psum | solution.py:99
  523.4 1.9 fusion.28
  525.3 1.3 dynamic-slice
  527.3 192.7 %all-reduce.9.cloned.1.call-done = f32[128,512]{1,0:T(8,128)} async-done(((f32[128,512]{1,0:T(8,128)}), f32[128,512]{1,0:T(8,128)}) %all-reduce.9.cloned.1.call-update) | async-done | bytes 262160
  720.0 1.3 fusion.43
  (57 shorter events, 7.5 us)
Async XLA Ops:
  7.2 446.1 %copy-start = (bf16[512,384]{1,0:T(8,128)(2,1)S(1)}, bf16[512,384]{1,0:T(8,128)(2,1)}, u32[]{:S(2)}) copy-start(bf16[512,384]{1,0:T(8,128)(2,1)} %param.20) | copy-start | bytes 1179652
  85.5 15.3 %all-to-all-start.1 = ((f32[64,2,8]{2,1,0:T(2,128)}), f32[64,2,8]{2,1,0:T(2,128)S(1)}, u32[]{:S(2)}, u32[]{:S(2)}) async-start(f32[64,2,8]{2,1,0:T(2,128)} %bitcast.4), calls=%async_computation.1 | async-start | bytes 131072 | tf_op jit(solution)/shard_map/all_to_all | solution.py:48
  100.8 13.8 %all-to-all-start = ((f32[64,1,128]{2,1,0:T(1,128)}), f32[64,1,128]{2,1,0:T(1,128)S(1)}, u32[]{:S(2)}, u32[]{:S(2)}) async-start(f32[64,1,128]{2,1,0:T(1,128)} %reshape.85), calls=%async_computation | async-start | bytes 65536 | tf_op jit(solution)/shard_map/all_to_all | solution.py:47
  105.2 36.1 %reduce-scatter.12.cloned.1.call-start = ((), (), s32[]{:S(2)}) async-start(), calls=%async_computation.9 | async-start | bytes 294912
  106.4 82.9 %reduce-scatter.10.cloned.1.call-start = ((), (), s32[]{:S(2)}) async-start(), calls=%async_computation.8 | async-start | bytes 2359296
  116.0 2.2 copy-start.7
  116.0 74.5 %copy-start.2 = (bf16[2,2,32,2048]{3,2,1,0:T(8,128)(2,1)S(1)}, bf16[2,2,32,2048]{3,2,1,0:T(8,128)(2,1)}, u32[]{:S(2)}) copy-start(bf16[2,2,32,2048]{3,2,1,0:T(8,128)(2,1)} %param.15) | copy-start | bytes 1572868
  118.0 210.5 %copy-start.3 = (bf16[512,64]{0,1:T(8,128)(2,1)S(1)}, bf16[512,64]{0,1:T(8,128)(2,1)}, u32[]{:S(2)}) copy-start(bf16[512,64]{0,1:T(8,128)(2,1)} %param.18) | copy-start | bytes 196612
  118.1 149.8 %all-reduce.5.cloned.1.call-start = ((), (), s32[]{:S(2)}) async-start(), calls=%async_computation.6 | async-start | bytes 524288 | tf_op jit(solution)/shard_map/psum | solution.py:64
  142.2 205.6 %copy-start.5 = (bf16[2,64]{1,0:T(2,128)(2,1)}, bf16[2,64]{1,0:T(2,128)(2,1)S(1)}, u32[]{:S(2)}) copy-start(bf16[2,64]{1,0:T(2,128)(2,1)S(1)} %copy.36) | copy-start | bytes 772
  191.4 188.9 %reduce-scatter.14.cloned.1.call-start = ((), (), s32[]{:S(2)}) async-start(), calls=%async_computation.10 | async-start | bytes 2359296
  345.7 35.6 %copy-start.4 = (bf16[2,512]{1,0:T(2,128)(2,1)S(1)}, bf16[2,512]{1,0:T(2,128)(2,1)}, u32[]{:S(2)}) copy-start(bf16[2,512]{1,0:T(2,128)(2,1)} %param.11) | copy-start | bytes 6148
  345.8 47.8 %copy-start.6 = (f32[512]{0:T(512)S(1)}, f32[512]{0:T(512)}, u32[]{:S(2)}) copy-start(f32[512]{0:T(512)} %param.19) | copy-start | bytes 6148
  347.8 175.6 %copy-start.1 = (bf16[192,512]{1,0:T(8,128)(2,1)S(1)}, bf16[192,512]{1,0:T(8,128)(2,1)}, u32[]{:S(2)}) copy-start(bf16[192,512]{1,0:T(8,128)(2,1)} %param.21) | copy-start | bytes 589828
  347.8 175.6 %all-reduce.7.cloned.1.call-start = ((), (), s32[]{:S(2)}) async-start(), calls=%async_computation.7 | async-start | bytes 393216 | tf_op jit(solution)/shard_map/psum | solution.py:99
  454.2 265.8 %all-reduce.9.cloned.1.call-start = ((), (), s32[]{:S(2)}) async-start(), calls=%async_computation.11 | async-start | bytes 524288
Sparse Core Ops, SparseCore 0:
  108.8 32.4 reduce-scatter.11
  144.2 45.0 reduce-scatter.9
  191.6 76.2 all-reduce.4
  348.0 32.2 reduce-scatter.13
  454.3 69.0 all-reduce.6
  526.7 193.2 all-reduce.8
where the time goes:
time: 729 us; the launch traced here: 728 us
  waiting for transfers between devices  446 us (61%)
  blocking collectives  231 us (32%)
  between operations  15 us (2%)
  local copies, waits for them, and re-layouts  12.2 us (2%)
  starting transfers between devices  10.2 us (1%)
  other arithmetic  7.74 us (1%)
    unnamed x10, waiting for transfers between devices  295 us
    psum x1, waiting for transfers between devices, body(): ffn_total = lax.psum(ffn_parts, 'ch')  69.2 us
    psum x1, waiting for transfers between devices, body(): summed, own_sum = lax.psum((score_part, own_part), 'ch')  64.4 us
    all_gather x1, blocking collectives, body(): lax.all_gather(normed, 'req', axis=0, tiled=True)  60.2 us
    all_gather x1, blocking collectives, body(): lax.all_gather(normed_two, 'req', axis=0, tiled=True)  59.6 us
    all_gather x1, blocking collectives, body(): lax.all_gather(attn_local, 'req', axis=0, tiled=True)  57 us
    psum x2, blocking collectives, rms_norm(): summed = lax.psum(squares, 'ch')  26.7 us
    all_to_all x1, blocking collectives, body(): lax.all_to_all(out_parts, 'req', split_axis=0, concat_axis=1, tiled=True)  16.1 us
  transfers between devices with their start and end apart: 8, of which 8 were waited for; matrix products, arithmetic and copies ran while one was open for 1% of the time, Pallas kernels for 0%

commit v1 on v0

--- a/solution.py
+++ b/solution.py
@@ -38,7 +38,12 @@
     normed = rms_norm(tokens, attn_gain)
     joined = jnp.concatenate([w_query, w_keyval], axis=1)
     head_parts = jnp.dot(
-        lax.all_gather(normed, "req", axis=0, tiled=True),
+        jnp.concatenate(
+            jax.lax.all_to_all(
+                jnp.stack([normed for _ in range(jax.lax.axis_size("req"))], axis=0), "req", 0, 0
+            ),
+            axis=0,
+        ),
         joined,
         preferred_element_type=jnp.float32,
     )

time: 729 us -> 696 us (0.955)
  blocking collectives: 231 us -> 199 us
    all_gather x1 -> x0, blocking collectives: 60.2 us -> none  [body(): lax.all_gather(normed, 'req', axis=0, tiled=True)]
    all_to_all x0 -> x1, blocking collectives: none -> 27.9 us  [body(): jax.lax.all_to_all(jnp.stack([normed for _ in range(jax.lax.axis_size('re...]
where the time goes in v1:
time: 696 us; the launch traced here: 695 us
  waiting for transfers between devices  446 us (64%)
  blocking collectives  199 us (29%)
  between operations  15 us (2%)
  local copies, waits for them, and re-layouts  12.3 us (2%)
  starting transfers between devices  9.49 us (1%)
  other arithmetic  7.74 us (1%)
    unnamed x10, waiting for transfers between devices  296 us
    psum x1, waiting for transfers between devices, body(): ffn_total = lax.psum(ffn_parts, 'ch')  69.1 us
    psum x1, waiting for transfers between devices, body(): summed, own_sum = lax.psum((score_part, own_part), 'ch')  64.5 us
    all_gather x1, blocking collectives, body(): lax.all_gather(normed_two, 'req', axis=0, tiled=True)  59.8 us
    all_gather x1, blocking collectives, body(): lax.all_gather(attn_local, 'req', axis=0, tiled=True)  57 us
    all_to_all x1, blocking collectives, body(): jax.lax.all_to_all(jnp.stack([normed for _ in range(jax.lax.axis_size('re...  27.9 us
    psum x2, blocking collectives, rms_norm(): summed = lax.psum(squares, 'ch')  26.5 us
    all_to_all x1, blocking collectives, body(): lax.all_to_all(out_parts, 'req', split_axis=0, concat_axis=1, tiled=True)  16.1 us
  transfers between devices with their start and end apart: 8, of which 8 were waited for; matrix products, arithmetic and copies ran while one was open for 1% of the time, Pallas kernels for 0%

profile of v1, /device:TPU:1, one launch (start us, length us, event | category | flops | bytes accessed | tf_op | source)
XLA Modules:
  0.0 695.2 jit_solution(9891826642196067593)
XLA Ops:
  7.2 0.8 fusion.36
  8.0 14.7 %psum.35 = f32[2]{0:T(128)S(1)} all-reduce(f32[2]{0:T(128)S(1)} %fusion.36), channel_id=1, replica_groups=mesh['req'=64,'ch'=8] {'ch'}, use_global_device_ids=true, to_apply=%region_1.0 | all-reduce | flops 2 | bytes 16 | tf_op jit(solution)/shard_map/psum | solution.py:16
  23.6 27.9 %all_to_all.62 = bf16[64,2,512]{2,1,0:T(2,128)(2,1)S(1)} all-to-all(bf16[64,2,512]{2,1,0:T(2,128)(2,1)S(1)} %stack.2), channel_id=1, replica_groups=mesh['req'=64,'ch'=8] {'req'}, dimensions={0} | all-to-all | bytes 262144 | tf_op jit(solution)/shard_map/all_to_all | solution.py:42
  51.5 1.0 fusion.24
  53.3 4.9 all-to-all-start.2
  59.0 8.9 %all-to-all-done.2 = f32[64,2,8]{2,1,0:T(2,128)S(1)} async-done(((f32[64,2,8]{2,1,0:T(2,128)}), f32[64,2,8]{2,1,0:T(2,128)S(1)}, u32[]{:S(2)}, u32[]{:S(2)}) %all-to-all-start.2) | async-done | bytes 4128 | tf_op jit(solution)/shard_map/all_to_all | solution.py:53
  68.0 4.4 all-to-all-start.1
  72.4 1.2 copy.40
  74.3 7.5 %all-to-all-done.1 = f32[64,1,128]{2,1,0:T(1,128)S(1)} async-done(((f32[64,1,128]{2,1,0:T(1,128)}), f32[64,1,128]{2,1,0:T(1,128)S(1)}, u32[]{:S(2)}, u32[]{:S(2)}) %all-to-all-start.1) | async-done | bytes 32800 | tf_op jit(solution)/shard_map/all_to_all | solution.py:52
  83.1 2.0 copy.39
  85.4 23.1 %reduce-scatter.12.cloned.1.call-done = f32[64,2]{1,0:T(8,128)} async-done(((f32[512,2]{1,0:T(8,128)}), f32[64,2]{1,0:T(8,128)}) %reduce-scatter.12.cloned.1.call-update) | async-done | bytes 528
  109.3 47.2 %reduce-scatter.10.cloned.1.call-done = f32[512,2]{1,0:T(8,128)} async-done(((f32[4096,2]{1,0:T(8,128)}), f32[512,2]{1,0:T(8,128)}) %reduce-scatter.10.cloned.1.call-update) | async-done | bytes 4112
  156.5 1.1 copy.34
  157.7 0.9 fusion.3
  158.8 11.8 %psum.37 = f32[2,16]{1,0:T(2,128)S(1)} all-reduce(f32[2,16]{1,0:T(2,128)S(1)} %multiply_reduce_fusion), channel_id=1, replica_groups=mesh['req'=64,'ch'=8] {'ch'}, use_global_device_ids=true, to_apply=%region_7.8 | all-reduce | flops 32 | bytes 256 | tf_op jit(solution)/shard_map/psum | solution.py:69
  170.6 64.5 %all-reduce.5.cloned.1.call-done = f32[2,16,2048]{2,1,0:T(8,128)} async-done(((f32[2,16,2048]{2,1,0:T(8,128)}), f32[2,16,2048]{2,1,0:T(8,128)}) %all-reduce.5.cloned.1.call-update) | async-done | bytes 262160 | tf_op jit(solution)/shard_map/psum | solution.py:69
  235.0 1.1 fusion.7
  236.1 1.2 fusion.8
  237.3 1.2 fusion.1
  238.6 57.0 %all-gather = bf16[64,2,512]{2,1,0:T(2,128)(2,1)S(1)} all-gather(bf16[1,2,512]{2,1,0:T(2,128)(2,1)S(1)} %reshape.77), channel_id=1, replica_groups=mesh['req'=64,'ch'=8] {'req'}, dimensions={0}, use_global_device_ids=true | all-gather | bytes 133120 | tf_op jit(solution)/shard_map/all_gather | solution.py:90
  295.9 16.1 %all_to_all.63 = f32[64,1,128]{2,1,0:T(1,128)S(1)} all-to-all(f32[64,1,128]{2,1,0:T(1,128)S(1)} %reshape.91), channel_id=1, replica_groups=mesh['req'=64,'ch'=8] {'req'}, dimensions={0} | all-to-all | bytes 65536 | tf_op jit(solution)/shard_map/all_to_all | solution.py:94
  312.9 2.0 copy.41
  315.0 32.4 %reduce-scatter.14.cloned.1.call-done = f32[512,2]{1,0:T(8,128)} async-done(((f32[4096,2]{1,0:T(8,128)}), f32[512,2]{1,0:T(8,128)}) %reduce-scatter.14.cloned.1.call-update) | async-done | bytes 4112
  347.4 1.1 copy.38
  348.6 11.8 %psum.38 = f32[2]{0:T(128)S(1)} all-reduce(f32[2]{0:T(128)S(1)} %get-tuple-element.2), channel_id=1, replica_groups=mesh['req'=64,'ch'=8] {'ch'}, use_global_device_ids=true, to_apply=%region_11.12 | all-reduce | flops 2 | bytes 16 | tf_op jit(solution)/shard_map/psum | solution.py:16
  360.5 59.8 %all-gather.1 = bf16[64,2,512]{2,1,0:T(2,128)(2,1)S(1)} all-gather(bf16[1,2,512]{2,1,0:T(2,128)(2,1)S(1)} %fusion.44), channel_id=1, replica_groups=mesh['req'=64,'ch'=8] {'req'}, dimensions={0}, use_global_device_ids=true | all-gather | bytes 133120 | tf_op jit(solution)/shard_map/all_gather | solution.py:100
  420.4 0.9 fusion.55
  421.4 69.1 %all-reduce.7.cloned.1.call-done = f32[128,384]{1,0:T(8,128)} async-done(((f32[128,384]{1,0:T(8,128)}), f32[128,384]{1,0:T(8,128)}) %all-reduce.7.cloned.1.call-update) | async-done | bytes 196624 | tf_op jit(solution)/shard_map/psum | solution.py:104
  490.5 1.9 fusion.28
  492.4 1.3 dynamic-slice
  494.3 192.7 %all-reduce.9.cloned.1.call-done = f32[128,512]{1,0:T(8,128)} async-done(((f32[128,512]{1,0:T(8,128)}), f32[128,512]{1,0:T(8,128)}) %all-reduce.9.cloned.1.call-update) | async-done | bytes 262160
  687.1 1.3 fusion.43
  (58 shorter events, 7.5 us)
Async XLA Ops:
  7.2 413.2 %copy-start = (bf16[512,384]{1,0:T(8,128)(2,1)S(1)}, bf16[512,384]{1,0:T(8,128)(2,1)}, u32[]{:S(2)}) copy-start(bf16[512,384]{1,0:T(8,128)(2,1)} %param.20) | copy-start | bytes 1179652
  53.3 14.7 %all-to-all-start.2 = ((f32[64,2,8]{2,1,0:T(2,128)}), f32[64,2,8]{2,1,0:T(2,128)S(1)}, u32[]{:S(2)}, u32[]{:S(2)}) async-start(f32[64,2,8]{2,1,0:T(2,128)} %bitcast.3), calls=%async_computation.2 | async-start | bytes 131072 | tf_op jit(solution)/shard_map/all_to_all | solution.py:53
  68.0 13.8 %all-to-all-start.1 = ((f32[64,1,128]{2,1,0:T(1,128)}), f32[64,1,128]{2,1,0:T(1,128)S(1)}, u32[]{:S(2)}, u32[]{:S(2)}) async-start(f32[64,1,128]{2,1,0:T(1,128)} %reshape.89), calls=%async_computation.1 | async-start | bytes 65536 | tf_op jit(solution)/shard_map/all_to_all | solution.py:52
  72.3 36.1 %reduce-scatter.12.cloned.1.call-start = ((), (), s32[]{:S(2)}) async-start(), calls=%async_computation.10 | async-start | bytes 294912
  73.6 83.0 %reduce-scatter.10.cloned.1.call-start = ((), (), s32[]{:S(2)}) async-start(), calls=%async_computation.9 | async-start | bytes 2359296
  83.1 2.1 copy-start.7
  83.1 74.6 %copy-start.2 = (bf16[2,2,32,2048]{3,2,1,0:T(8,128)(2,1)S(1)}, bf16[2,2,32,2048]{3,2,1,0:T(8,128)(2,1)}, u32[]{:S(2)}) copy-start(bf16[2,2,32,2048]{3,2,1,0:T(8,128)(2,1)} %param.15) | copy-start | bytes 1572868
  85.2 210.5 %copy-start.3 = (bf16[512,64]{0,1:T(8,128)(2,1)S(1)}, bf16[512,64]{0,1:T(8,128)(2,1)}, u32[]{:S(2)}) copy-start(bf16[512,64]{0,1:T(8,128)(2,1)} %param.18) | copy-start | bytes 196612
  85.2 149.8 %all-reduce.5.cloned.1.call-start = ((), (), s32[]{:S(2)}) async-start(), calls=%async_computation.7 | async-start | bytes 524288 | tf_op jit(solution)/shard_map/psum | solution.py:69
  109.3 205.6 %copy-start.5 = (bf16[2,64]{1,0:T(2,128)(2,1)}, bf16[2,64]{1,0:T(2,128)(2,1)S(1)}, u32[]{:S(2)}) copy-start(bf16[2,64]{1,0:T(2,128)(2,1)S(1)} %copy.36) | copy-start | bytes 772
  158.6 188.9 %reduce-scatter.14.cloned.1.call-start = ((), (), s32[]{:S(2)}) async-start(), calls=%async_computation.11 | async-start | bytes 2359296
  312.9 35.6 %copy-start.4 = (bf16[2,512]{1,0:T(2,128)(2,1)S(1)}, bf16[2,512]{1,0:T(2,128)(2,1)}, u32[]{:S(2)}) copy-start(bf16[2,512]{1,0:T(2,128)(2,1)} %param.11) | copy-start | bytes 6148
  312.9 47.6 %copy-start.6 = (f32[512]{0:T(512)S(1)}, f32[512]{0:T(512)}, u32[]{:S(2)}) copy-start(f32[512]{0:T(512)} %param.19) | copy-start | bytes 6148
  314.9 175.5 %copy-start.1 = (bf16[192,512]{1,0:T(8,128)(2,1)S(1)}, bf16[192,512]{1,0:T(8,128)(2,1)}, u32[]{:S(2)}) copy-start(bf16[192,512]{1,0:T(8,128)(2,1)} %param.21) | copy-start | bytes 589828
  315.0 175.5 %all-reduce.7.cloned.1.call-start = ((), (), s32[]{:S(2)}) async-start(), calls=%async_computation.8 | async-start | bytes 393216 | tf_op jit(solution)/shard_map/psum | solution.py:104
  421.3 265.7 %all-reduce.9.cloned.1.call-start = ((), (), s32[]{:S(2)}) async-start(), calls=%async_computation.12 | async-start | bytes 524288
Sparse Core Ops, SparseCore 0:
  75.9 32.4 reduce-scatter.11
  111.3 45.1 reduce-scatter.9
  158.8 76.1 all-reduce.4
  315.1 32.2 reduce-scatter.13
  421.4 68.9 all-reduce.6
  493.8 193.2 all-reduce.8
